TPU v7x, 128 devices: a whole 4x4x4 slice. The times are simulated.
128 devices in a mesh: row: 4 (over x_lo, core), col: 32 (over y, z, x_hi).
Axes of the slice: x: 4 (x_hi: 2, x_lo: 2; x = x_hi * 2 + x_lo), y: 4, z: 4, core: 2. Of those that a mesh axis runs over, the one named last changes fastest.
Arguments:
- prompt_tokens: bfloat16 [32768, 2048], P('col', 'row'), may hold values from -6 to 6
- decode_tokens: bfloat16 [32, 2048], P('col', 'row'), may hold values from -6 to 6
- norm_gain: float32 [2048], replicated, may hold values from 0.25 to 1.75
- norm_bias: float32 [2048], replicated, may hold values from -3 to 3
- project_weight: float32 [2048, 6144], P(('row', 'col')), may hold values from -0.25 to 0.25
- dense_weight: float32 [2048, 2048], P(('row', 'col')), may hold values from -0.125 to 0.125
- expand_weight: float32 [2048, 8192], P(('row', 'col')), may hold values from -0.125 to 0.125
- reduce_weight: float32 [2048, 8192], P(('row', 'col')), may hold values from -0.0625 to 0.0625
- key_cache: bfloat16 [32, 32, 262144], P('col', 'row'), may hold values from -15 to 15
- value_cache: bfloat16 [32, 32, 262144], P('col', 'row'), may hold values from -12 to 12
- prompt_lengths: int32 [64], P('col'), may hold values from 128 to 512, as said below
- cache_ages: int32 [32], replicated, may hold values from 1 to 4096, as said below
- slot_request: int32 [32], replicated, may hold values from 0 to 31, each once
Outputs:
- prompt_out: bfloat16 [32768, 2048], P('col', 'row')
- decoded: bfloat16 [32, 2048], P('col', 'row')
Inputs may be any that keep to these rules, and one draw needn't show every extreme that they name: `prompt_lengths`: tokens of a prompt at or beyond its length are padding; some prompt is full in every draw. `cache_ages`: cached positions 0 to age - 1 of a request are valid and its new token stands at position age; some request has exactly 4096. `slot_request`: a permutation of the requests.
All inputs are finite; a program needn't handle non-finite values.
Results may differ from a plain program's by a relative error of at most 0.012.
The roundings to bfloat16 on the way count: a program that leaves them out, or rounds other values in their place, can miss the bound.
Values may be sent and summed in bfloat16 or wider, within the bound.
No kernel may reach another device: no remote copies, remote signals or barrier semaphores. Data moves between devices by JAX's collectives and lax.ppermute only.
A program may use at most 192 MiB of HBM per device.

v0:
```python
import jax
import jax.numpy as jnp
from jax import lax
from jax.sharding import PartitionSpec as P

HD = 64
ROT = 32
PLEN = 512
CTX = 4096
KEY_BLOCK = 512
NEG = -1e30


def layer_norm(rows, gain, bias):
    values = rows.astype(jnp.float32)
    centre = jnp.mean(values, axis=-1, keepdims=True)
    centred = values - centre
    deviation = jnp.mean(centred * centred, axis=-1, keepdims=True)
    return (centred * lax.rsqrt(deviation + 1e-05) * gain + bias).astype(jnp.bfloat16)


def rotary(vectors, position):
    half_width = ROT // 2
    frequency = 10000.0 ** (-2.0 * jnp.arange(half_width).astype(jnp.float32) / ROT)
    angle = position.astype(jnp.float32)[..., None, None] * frequency
    cosine = jnp.cos(angle)
    sine_value = jnp.sin(angle)
    lower_part = vectors[..., :half_width]
    upper_part = vectors[..., half_width:ROT]
    return jnp.concatenate(
        [
            lower_part * cosine - upper_part * sine_value,
            upper_part * cosine + lower_part * sine_value,
            vectors[..., ROT:],
        ],
        axis=-1,
    )


def restore_rows(block, row_count, col_count):
    width = block.shape[1]
    shard_rows = block.shape[0] // (row_count * col_count)
    return (
        block.reshape(col_count, row_count, shard_rows, width)
        .transpose(1, 0, 2, 3)
        .reshape(row_count * col_count * shard_rows, width)
    )


def on_device(
    prompt_tokens,
    decode_tokens,
    norm_gain,
    norm_bias,
    project_weight,
    dense_weight,
    expand_weight,
    reduce_weight,
    key_cache,
    value_cache,
    prompt_lengths,
    cache_ages,
    slot_request,
):
    half_float = jnp.bfloat16
    row_count = lax.axis_size("row")
    col_count = lax.axis_size("col")
    regrouped = (
        lax.all_to_all(
            project_weight.astype(half_float), "row", split_axis=1, concat_axis=0, tiled=True
        ),
        lax.all_to_all(
            dense_weight.astype(half_float), "row", split_axis=1, concat_axis=0, tiled=True
        ),
        lax.all_to_all(
            expand_weight.astype(half_float), "row", split_axis=1, concat_axis=0, tiled=True
        ),
        lax.all_to_all(
            reduce_weight.astype(half_float), "row", split_axis=1, concat_axis=0, tiled=True
        ),
    )
    gathered = (
        lax.all_gather(regrouped[0], "col", axis=0, tiled=True),
        lax.all_gather(regrouped[1], "col", axis=0, tiled=True),
        lax.all_gather(regrouped[2], "col", axis=0, tiled=True),
        lax.all_gather(regrouped[3], "col", axis=0, tiled=True),
    )
    w_project, w_dense, w_expand, w_reduce = [
        restore_rows(piece, row_count, col_count) for piece in gathered
    ]
    prompt_full, decode_full = (
        lax.all_gather(prompt_tokens, "row", axis=1, tiled=True),
        lax.all_gather(decode_tokens, "row", axis=1, tiled=True),
    )
    rows_prompt = prompt_full.shape[0]
    slot_local = decode_full.shape[0]
    prompt_count = rows_prompt // PLEN
    heads_local = w_dense.shape[1] // HD
    total_slots = slot_request.shape[0]
    scale = HD ** (-0.5)
    joined = jnp.concatenate([prompt_full, decode_full], axis=0)
    normed = layer_norm(joined, norm_gain, norm_bias)
    merged = jnp.dot(normed, w_project, preferred_element_type=jnp.float32)
    hidden = jax.nn.gelu(
        jnp.dot(normed, w_expand, preferred_element_type=jnp.float32), approximate=True
    ).astype(half_float)
    mlp_part = lax.dot_general(
        hidden, w_reduce, (((1,), (1,)), ((), ())), preferred_element_type=jnp.float32
    )
    places = jnp.arange(PLEN, dtype=jnp.int32)

    def prompt_block(items):
        block, length = items
        queries = rotary(block[:, :, 0], places).astype(half_float)
        keys_rot = rotary(block[:, :, 1], places).astype(half_float)
        values = block[:, :, 2].astype(half_float)
        scores = (
            jnp.einsum("qhd,khd->hqk", queries, keys_rot, preferred_element_type=jnp.float32)
            * scale
        )
        allowed = (places[None, :] <= places[:, None]) & (places[None, :] < length)
        scores = jnp.where(allowed[None], scores, NEG)
        top = jnp.max(scores, axis=-1, keepdims=True)
        raised = jnp.exp(scores - top)
        probs = (raised / jnp.sum(raised, axis=-1, keepdims=True)).astype(half_float)
        mixed = jnp.einsum("hqk,khd->qhd", probs, values, preferred_element_type=jnp.float32)
        return mixed.astype(half_float).reshape(PLEN, heads_local * HD)

    prompt_blocks = merged[:rows_prompt].reshape(prompt_count, PLEN, heads_local, 3, HD)
    prompt_mixed = lax.map(prompt_block, (prompt_blocks, prompt_lengths)).reshape(
        rows_prompt, heads_local * HD
    )
    col_index = lax.axis_index("col")
    first_slot = col_index * slot_local
    local_ids = first_slot + jnp.arange(slot_local, dtype=jnp.int32)
    own_request = lax.dynamic_slice_in_dim(slot_request, first_slot, slot_local)
    all_ids = jnp.arange(total_slots, dtype=jnp.int32)
    slot_match = own_request[:, None] == all_ids[None, :]
    slot_age = jnp.sum(jnp.where(slot_match, cache_ages[None, :], 0), axis=1)
    decode_pieces = merged[rows_prompt:].reshape(slot_local, heads_local, 3, HD)
    query_new = rotary(decode_pieces[:, :, 0], slot_age).astype(half_float)
    key_new = rotary(decode_pieces[:, :, 1], slot_age).astype(half_float)
    value_new = decode_pieces[:, :, 2].astype(half_float)
    packed = jnp.stack([query_new, key_new, value_new], axis=2).reshape(
        slot_local, heads_local * 3 * HD
    )
    handed = lax.all_gather(packed, "col", axis=0, tiled=True)
    chooser = (slot_request[None, :] == local_ids[:, None]).astype(half_float)
    mine = jnp.dot(chooser, handed, preferred_element_type=jnp.float32).astype(half_float)
    mine = mine.reshape(slot_local, heads_local, 3, HD)
    query = mine[:, :, 0]
    own_key = mine[:, :, 1]
    own_value = mine[:, :, 2]
    local_ages = lax.dynamic_slice_in_dim(cache_ages, first_slot, slot_local)
    keys_local = key_cache.reshape(slot_local, heads_local, CTX, HD)
    values_local = value_cache.reshape(slot_local, heads_local, CTX, HD)
    block_count = CTX // KEY_BLOCK

    def score_block(step, held):
        start = step * KEY_BLOCK
        keys_block = lax.dynamic_slice_in_dim(keys_local, start, KEY_BLOCK, 2)
        block_scores = (
            jnp.einsum("shd,shtd->sht", query, keys_block, preferred_element_type=jnp.float32)
            * scale
        )
        key_places = start + jnp.arange(KEY_BLOCK, dtype=jnp.int32)
        block_scores = jnp.where(
            key_places[None, None, :] < local_ages[:, None, None], block_scores, NEG
        )
        return lax.dynamic_update_slice_in_dim(held, block_scores, start, 2)

    cache_scores = lax.fori_loop(
        0, block_count, score_block, jnp.full((slot_local, heads_local, CTX), NEG, jnp.float32)
    )
    own_score = jnp.sum(query.astype(jnp.float32) * own_key.astype(jnp.float32), axis=-1) * scale
    decode_top = jnp.maximum(jnp.max(cache_scores, axis=-1), own_score)
    cache_raised = jnp.exp(cache_scores - decode_top[:, :, None])
    own_raised = jnp.exp(own_score - decode_top)
    decode_total = jnp.sum(cache_raised, axis=-1) + own_raised
    cache_probs = (cache_raised / decode_total[:, :, None]).astype(half_float)
    own_prob = (own_raised / decode_total).astype(half_float)

    def value_block(step, running):
        start = step * KEY_BLOCK
        probs_block = lax.dynamic_slice_in_dim(cache_probs, start, KEY_BLOCK, 2)
        values_block = lax.dynamic_slice_in_dim(values_local, start, KEY_BLOCK, 2)
        return running + jnp.einsum(
            "sht,shtd->shd", probs_block, values_block, preferred_element_type=jnp.float32
        )

    start_value = own_prob.astype(jnp.float32)[:, :, None] * own_value.astype(jnp.float32)
    decode_sum = lax.fori_loop(0, block_count, value_block, start_value)
    decode_mixed = decode_sum.astype(half_float).reshape(slot_local, heads_local * HD)
    returned = lax.all_gather(decode_mixed, "col", axis=0, tiled=True)
    picker = slot_match.astype(half_float)
    decode_heads = jnp.dot(picker, returned, preferred_element_type=jnp.float32).astype(half_float)
    mixed_all = jnp.concatenate([prompt_mixed, decode_heads], axis=0)
    attn_part = lax.dot_general(
        mixed_all, w_dense, (((1,), (1,)), ((), ())), preferred_element_type=jnp.float32
    )
    attn_prompt, attn_decode = (
        lax.psum_scatter(attn_part[:rows_prompt], "row", scatter_dimension=1, tiled=True),
        lax.psum_scatter(attn_part[rows_prompt:], "row", scatter_dimension=1, tiled=True),
    )
    mlp_prompt, mlp_decode = (
        lax.psum_scatter(
            mlp_part[:rows_prompt].astype(jnp.bfloat16), "row", scatter_dimension=1, tiled=True
        ).astype(jnp.float32),
        lax.psum_scatter(
            mlp_part[rows_prompt:].astype(jnp.bfloat16), "row", scatter_dimension=1, tiled=True
        ).astype(jnp.float32),
    )
    summed_prompt = attn_prompt + mlp_prompt
    summed_decode = attn_decode + mlp_decode
    prompt_result = prompt_tokens.astype(jnp.float32) + summed_prompt
    decode_result = decode_tokens.astype(jnp.float32) + summed_decode
    return (prompt_result.astype(half_float), decode_result.astype(half_float))


def solution(mesh):
    in_specs = (
        P("col", "row"),
        P("col", "row"),
        P(),
        P(),
        P(("row", "col"), None),
        P(("row", "col"), None),
        P(("row", "col"), None),
        P(("row", "col"), None),
        P("col", "row", None),
        P("col", "row", None),
        P("col"),
        P(),
        P(),
    )
    out_specs = (P("col", "row"), P("col", "row"))
    return jax.shard_map(
        on_device, mesh=mesh, in_specs=in_specs, out_specs=out_specs, check_vma=False
    )
```

profile of v0, /device:TPU:1, one launch (start us, length us, event | category | flops | bytes accessed | tf_op | source)
XLA Modules:
  0.0 743.6 jit_solution(17155492854786503554)
XLA Ops:
  8.1 7.7 %all_to_all.76 = bf16[16,4,512]{2,0,1:T(8,128)(2,1)} all-to-all(bf16[16,4,512]{2,0,1:T(8,128)(2,1)S(1)} %bitcast.183), channel_id=1, replica_groups=mesh['row'=4,'col'=32] {'row'}, dimensions={1} | all-to-all | bytes 131072 | tf_op jit(solution)/shard_map/all_to_all | solution.py:72
  17.7 8.5 %all_to_all.77 = bf16[16,4,1536]{2,0,1:T(8,128)(2,1)} all-to-all(bf16[16,4,1536]{2,0,1:T(8,128)(2,1)S(1)} %bitcast.177), channel_id=1, replica_groups=mesh['row'=4,'col'=32] {'row'}, dimensions={1} | all-to-all | bytes 393216 | tf_op jit(solution)/shard_map/all_to_all | solution.py:69
  27.4 8.8 %all_to_all.78 = bf16[16,4,2048]{2,0,1:T(8,128)(2,1)} all-to-all(bf16[16,4,2048]{2,0,1:T(8,128)(2,1)S(1)} %bitcast.175), channel_id=1, replica_groups=mesh['row'=4,'col'=32] {'row'}, dimensions={1} | all-to-all | bytes 524288 | tf_op jit(solution)/shard_map/all_to_all | solution.py:75
  38.0 4.4 all-to-all-start.3
  42.5 1.2 dynamic_slice.41
  43.7 1.3 dynamic_slice.42
  45.0 1.9 fusion.72
  47.6 6.1 reshape.576
  53.6 11.1 %reshape.545 = bf16[1,8,4096,64]{3,2,1,0:T(8,128)(2,1)} reshape(bf16[2097152]{0:T(1024)(128)(2,1)} %reshape.576) | data formatting | bytes 8388608 | tf_op jit(solution)/shard_map/reshape | solution.py:155
  64.7 6.0 reshape.578
  70.7 11.0 %reshape.546 = bf16[1,8,4096,64]{3,2,1,0:T(8,128)(2,1)} reshape(bf16[2097152]{0:T(1024)(128)(2,1)} %reshape.578) | data formatting | bytes 8388608 | tf_op jit(solution)/shard_map/reshape | solution.py:156
  81.8 5.1 all_gather.25
  88.2 3.2 copy.89
  91.4 44.8 %all-gather.8.cloned.1.call-done = bf16[1024,2048]{1,0:T(8,128)(2,1)} async-done(((bf16[1024,512]{1,0:T(8,128)(2,1)}), bf16[1024,2048]{1,0:T(8,128)(2,1)}) %all-gather.8.cloned.1.call-update) | async-done | bytes 4194320 | tf_op jit(solution)/shard_map/all_gather | solution.py:92
  136.2 2.8 convert_reduce_fusion
  139.1 3.0 fusion.36
  142.2 89.1 %all-gather.10.cloned.1.call-done = bf16[2048,1536]{1,0:T(8,128)(2,1)} async-done(((bf16[64,1536]{1,0:T(8,128)(2,1)}), bf16[2048,1536]{1,0:T(8,128)(2,1)}) %all-gather.10.cloned.1.call-update) | async-done | bytes 6291472 | tf_op jit(solution)/shard_map/all_gather | solution.py:83
  231.2 3.5 copy.76
  235.2 7.0 fusion.85
  242.2 3.1 slice.161
  245.4 6.6 copy.77
  252.0 9.2 %reshape.540 = f32[2,512,8,3,64]{1,0,4,3,2:T(2,128)} reshape(f32[1024,1536]{0,1:T(8,128)} %copy.77) | data formatting | bytes 12582912 | tf_op jit(solution)/shard_map/reshape | solution.py:129
  261.7 79.5 %all-gather = bf16[32,1,1536]{2,1,0:T(2,128)(2,1)S(1)} all-gather(bf16[1,1,1536]{2,1,0:T(2,128)(2,1)S(1)} %reshape.556), channel_id=1, replica_groups=mesh['row'=4,'col'=32] {'col'}, dimensions={0}, use_global_device_ids=true | all-gather | bytes 101376 | tf_op jit(solution)/shard_map/all_gather | solution.py:147
  341.6 18.2 %while.40 = (s32[]{:T(128)}, f32[1,8,4096]{2,1,0:T(8,128)S(1)}, s32[1]{0:T(128)}, bf16[1,8,4096,64]{3,2,1,0:T(8,128)(2,1)}, bf16[1,8,64]{2,1,0:T(8,128)(2,1)S(1)...) while((s32[]{:T(128)}, f32[1,8,4096]{2,1,0:T(8,128)S(1)}, s32[1]{0:T(128)}, ...), condition=%wide.region_9.10_spmd, body=%wide.region_8.9_spmd.sunk | while | flops 533510 | bytes 1099931 | solution.py:172
  342.3 1.6 fusion.110
  344.5 1.6 fusion.110
  346.8 1.6 fusion.110
  349.1 1.6 fusion.110
  351.4 1.6 fusion.110
  353.7 1.6 fusion.110
  355.9 1.6 fusion.110
  358.2 1.6 fusion.110
  360.4 12.2 %while.41 = (s32[]{:T(128)}, f32[1,8,64]{2,1,0:T(8,128)S(1)}, bf16[1,8,4096]{2,1,0:T(8,128)(2,1)S(1)}, bf16[1,8,4096,64]{3,2,1,0:T(8,128)(2,1)}, s32[]{:T(128)}, /*index=5*/s32[]{:T(128)}, s32[]{:T(128)}, s32[]{:T(128)}) while((s32[]{:T(128)}, f32[1,8,64]{2,1,0:T(8,128)S(1)}, bf16[1,8,4096]{2,1,0:T(8,128)(2,1)S(1)}, ...), condition=%wide.region_13.14_spmd, body=%wide.region_12.13_spmd.sunk | while | flops 524806 | bytes 1081483 | solution.py:192
  360.5 1.5 fusion.113
  362.0 1.5 fusion.113
  363.5 1.5 fusion.113
  365.0 1.5 fusion.113
  366.6 1.5 fusion.113
  368.1 1.5 fusion.113
  369.6 1.5 fusion.113
  371.1 1.5 fusion.113
  372.8 75.5 %all-gather.1 = bf16[32,1,512]{2,1,0:T(2,128)(2,1)S(1)} all-gather(bf16[1,1,512]{2,1,0:T(2,128)(2,1)S(1)} %reshape.558), channel_id=1, replica_groups=mesh['row'=4,'col'=32] {'col'}, dimensions={0}, use_global_device_ids=true | all-gather | bytes 33792 | tf_op jit(solution)/shard_map/all_gather | solution.py:194
  449.5 53.5 %while.42 = (s32[]{:T(128)}, bf16[2,512,512]{2,1,0:T(8,128)(2,1)}, f32[2,512,8,3,64]{1,0,4,3,2:T(2,128)}, s32[2]{0:T(128)}, s32[]{:T(128)}) while((s32[]{:T(128)}, bf16[2,512,512]{2,1,0:T(8,128)(2,1)}, f32[2,512,8,3,64]{1,0,4,3,2:T(2,128)}, s32[2]{0:T(128)}, s32[]{:T(128)}) %tuple.118), condition=%wide.region_5.6_spmd.clone.clone, body=%wide.region_2.5_spmd.clone.clone.sunk | while | flops 554444288 | bytes 41063644 | solution.py:130
  449.5 1.2 dynamic_slice.66
  451.7 6.1 constant_dynamic-slice_fusion.2
  460.8 8.3 %fusion.116 = (f32[8,512]{1,0:T(8,128)}, f32[8,512,512]{1,2,0:T(8,128)}) fusion(pred[512,512]{0,1:T(8,128)(4,1)S(1)} %fusion.115, bf16[512,8,32]{0,2,1:T(8,128)(2,1)} %slice.235, bf16[512,8,16]{0,2,1:T(8,128)(2,1)} %get-tuple-element.479, bf16[512,8,16]{0,2,1:T(8,128)(2,1)} %get-tuple-element.480, bf16[512,8,32]{0,2,1:T(8,128)(2,1)} %slice.236, ...), kind=kOutput, calls=%fused_computation.141.clone.1 | convolution fusion | flops 279970304 | bytes 9715712 | tf_op jit(solution)/shard_map/while/body/eval_jaxpr/sub | solution.py:124
  469.1 5.1 fusion.117
  474.2 1.3 copy.148
  478.4 6.1 constant_dynamic-slice_fusion.2
  487.6 8.3 %fusion.116 = (f32[8,512]{1,0:T(8,128)}, f32[8,512,512]{1,2,0:T(8,128)}) fusion(pred[512,512]{0,1:T(8,128)(4,1)S(1)} %fusion.115, bf16[512,8,32]{0,2,1:T(8,128)(2,1)} %slice.235, bf16[512,8,16]{0,2,1:T(8,128)(2,1)} %get-tuple-element.479, bf16[512,8,16]{0,2,1:T(8,128)(2,1)} %get-tuple-element.480, bf16[512,8,32]{0,2,1:T(8,128)(2,1)} %slice.236, ...), kind=kOutput, calls=%fused_computation.141.clone.1 | convolution fusion | flops 279970304 | bytes 9715712 | tf_op jit(solution)/shard_map/while/body/eval_jaxpr/sub | solution.py:124
  495.8 5.1 fusion.117
  500.9 1.3 copy.148
  503.0 4.3 fusion.53
  507.3 3.3 copy-done.1
  510.7 1.3 copy.99
  512.3 8.4 %copy.91 = bf16[32,4,16,2048]{3,2,0,1:T(8,128)(2,1)} copy(bf16[32,4,16,2048]{3,2,1,0:T(8,128)(2,1)} %bitcast.161) | data formatting | bytes 16777216 | tf_op jit(solution)/shard_map/reshape | solution.py:44
  520.8 8.4 %copy.93 = bf16[32,4,16,2048]{3,2,0,1:T(8,128)(2,1)} copy(bf16[32,4,16,2048]{3,2,1,0:T(8,128)(2,1)} %bitcast.162) | data formatting | bytes 16777216 | tf_op jit(solution)/shard_map/reshape | solution.py:44
  529.2 27.6 %convolution_convert_fusion = bf16[1025,2048]{1,0:T(8,128)(2,1)} fusion(bf16[2048,2048]{1,0:T(8,128)(2,1)} %bitcast.164, bf16[2048,2048]{1,0:T(8,128)(2,1)} %bitcast.163, f32[2048]{0:T(1024)S(1)} %copy-done.9, f32[2048]{0:T(1024)S(1)} %copy-done.11, f32[1025]{0:T(1024)S(1)} %copy-done.5, f32[1025]{0:T(1024)S(1)} %broadcast_multiply_fusion, ...), kind=kOutput, calls=%fused_computation.73 | convolution fusion | flops 17236531200 | bytes 25198600 | tf_op jit(solution)/shard_map/dot_general | solution.py:107
  558.7 4.7 slice.170
  563.5 7.8 %slice.169 = f32[1024,2048]{1,0:T(8,128)} slice(f32[1025,2048]{1,0:T(8,128)} %copy-done.1), slice={[0:1024], [0:2048]} | slice | bytes 16777216 | tf_op jit(solution)/shard_map/slice | solution.py:202
  572.5 30.1 %reduce-scatter.15.cloned.1.call-done = bf16[512,1]{1,0:T(8,128)(2,1)} async-done(((bf16[2048,1]{1,0:T(8,128)(2,1)}), bf16[512,1]{1,0:T(8,128)(2,1)}) %reduce-scatter.15.cloned.1.call-update) | async-done | bytes 1040
  604.2 46.9 %reduce-scatter.11.cloned.1.call-done = bf16[1024,512]{1,0:T(8,128)(2,1)} async-done(((bf16[1024,2048]{1,0:T(8,128)(2,1)}), bf16[1024,512]{1,0:T(8,128)(2,1)}) %reduce-scatter.11.cloned.1.call-update) | async-done | bytes 1048592 | tf_op jit(solution)/shard_map/reduce_scatter | solution.py:206
  651.1 82.5 %reduce-scatter.9.cloned.1.call-done = f32[1024,512]{1,0:T(8,128)} async-done(((f32[1024,2048]{1,0:T(8,128)}), f32[1024,512]{1,0:T(8,128)}) %reduce-scatter.9.cloned.1.call-update) | async-done | bytes 2097168 | tf_op jit(solution)/shard_map/reduce_scatter | solution.py:202
  733.6 3.3 add_convert_fusion.2
  (154 shorter events, 31.8 us)
Async XLA Ops:
  7.2 81.1 %all-gather.12.cloned.1.call-start = ((), (), s32[]{:S(2)}) async-start(), calls=%async_computation.10 | async-start | bytes 2162688 | tf_op jit(solution)/shard_map/all_gather | solution.py:84
  15.9 120.4 %all-gather.8.cloned.1.call-start = ((), (), s32[]{:S(2)}) async-start(), calls=%async_computation.8 | async-start | bytes 5242880 | tf_op jit(solution)/shard_map/all_gather | solution.py:92
  16.6 214.6 %all-gather.10.cloned.1.call-start = ((), (), s32[]{:S(2)}) async-start(), calls=%async_computation.9 | async-start | bytes 6488064 | tf_op jit(solution)/shard_map/all_gather | solution.py:83
  26.3 486.1 %all-gather.14.cloned.1.call-start = ((), (), s32[]{:S(2)}) async-start(), calls=%async_computation.12 | async-start | bytes 8650752 | tf_op jit(solution)/shard_map/all_gather | solution.py:85
  38.0 48.9 %all-to-all-start.3 = ((bf16[16,4,2048]{2,0,1:T(8,128)(2,1)}), bf16[16,4,2048]{2,0,1:T(8,128)(2,1)S(1)}, u32[]{:S(2)}, u32[]{:S(2)}) async-start(bf16[16,4,2048]{2,0,1:T(8,128)(2,1)} %bitcast.126), calls=%async_computation.4 | async-start | bytes 524288 | tf_op jit(solution)/shard_map/all_to_all | solution.py:78
  42.5 478.3 %all-gather.16.cloned.1.call-start = ((), (), s32[]{:S(2)}) async-start(), calls=%async_computation.13 | async-start | bytes 8650752 | tf_op jit(solution)/shard_map/all_gather | solution.py:86
  64.7 17.1 %copy-start.6 = (bf16[1,512]{1,0:T(2,128)(2,1)S(1)}, bf16[1,512]{1,0:T(2,128)(2,1)}, u32[]{:S(2)}) copy-start(bf16[1,512]{1,0:T(2,128)(2,1)} %param.20) | copy-start | bytes 3076
  87.0 0.7 copy-start.3
  87.7 483.7 %reduce-scatter.13.cloned.1.call-start = ((), (), s32[]{:S(2)}) async-start(), calls=%async_computation.15 | async-start | bytes 1310720
  139.1 95.6 %copy-start.8 = (f32[2048]{0:T(1024)S(1)}, f32[2048]{0:T(1024)}, u32[]{:S(2)}) copy-start(f32[2048]{0:T(1024)} %param.22) | copy-start | bytes 24580
  139.1 95.6 %copy-start.10 = (f32[2048]{0:T(1024)S(1)}, f32[2048]{0:T(1024)}, u32[]{:S(2)}) copy-start(f32[2048]{0:T(1024)} %param.21) | copy-start | bytes 24580
  142.2 92.5 %copy-start.4 = (f32[1025]{0:T(1024)}, f32[1025]{0:T(1024)S(1)}, u32[]{:S(2)}) copy-start(f32[1025]{0:T(1024)S(1)} %add_rsqrt_fusion) | copy-start | bytes 12304
  231.2 4.0 copy-start
  252.0 89.2 %copy-start.12 = (s32[32]{0:T(128)S(1)}, s32[32]{0:T(128)}, u32[]{:S(2)}) copy-start(s32[32]{0:T(128)} %param.31) | copy-start | bytes 388
  507.3 3.3 copy-start.1
  512.1 90.5 %reduce-scatter.15.cloned.1.call-start = ((), (), s32[]{:S(2)}) async-start(), calls=%async_computation.16 | async-start | bytes 655360
  520.8 8.4 %copy-start.5 = (f32[1025]{0:T(1024)S(1)}, f32[1025]{0:T(1024)}, u32[]{:S(2)}) copy-start(f32[1025]{0:T(1024)} %copy-done.4) | copy-start | bytes 12304
  520.8 8.4 %copy-start.9 = (f32[2048]{0:T(1024)S(1)}, f32[2048]{0:T(1024)}, u32[]{:S(2)}) copy-start(f32[2048]{0:T(1024)} %param.22) | copy-start | bytes 24580
  520.8 8.4 %copy-start.11 = (f32[2048]{0:T(1024)S(1)}, f32[2048]{0:T(1024)}, u32[]{:S(2)}) copy-start(f32[2048]{0:T(1024)} %param.21) | copy-start | bytes 24580
  558.6 92.5 %reduce-scatter.11.cloned.1.call-start = ((), (), s32[]{:S(2)}) async-start(), calls=%async_computation.14 | async-start | bytes 5242880 | tf_op jit(solution)/shard_map/reduce_scatter | solution.py:206
  563.4 170.2 %reduce-scatter.9.cloned.1.call-start = ((), (), s32[]{:S(2)}) async-start(), calls=%async_computation.11 | async-start | bytes 10485760 | tf_op jit(solution)/shard_map/reduce_scatter | solution.py:202
  571.3 32.3 %copy-start.7 = (bf16[1,512]{1,0:T(2,128)(2,1)S(1)}, bf16[1,512]{1,0:T(2,128)(2,1)}, u32[]{:S(2)}) copy-start(bf16[1,512]{1,0:T(2,128)(2,1)} %param.20) | copy-start | bytes 3076
  571.3 162.3 %copy-start.2 = (bf16[1024,512]{1,0:T(8,128)(2,1)S(1)}, bf16[1024,512]{1,0:T(8,128)(2,1)}, u32[]{:S(2)}) copy-start(bf16[1024,512]{1,0:T(8,128)(2,1)} %param.19) | copy-start | bytes 3145732
Sparse Core Ops, SparseCore 0:
  16.0 71.9 all-gather.11
  89.6 46.5 all-gather.7
  139.2 91.9 all-gather.9
  234.2 104.1 all-gather.13
  341.4 102.0 all-gather.15
  512.2 45.2 reduce-scatter.12
  560.0 42.5 reduce-scatter.14
  605.1 45.9 reduce-scatter.10
  653.6 79.9 reduce-scatter.8
where the time goes:
time: 751 us; the launch traced here: 744 us
  waiting for transfers between devices  294 us (39%)
  blocking collectives  185 us (25%)
  local copies, waits for them, and re-layouts  127 us (17%)
  matrix products  91.1 us (12%)
  other arithmetic  25.6 us (3%)
  between operations  15 us (2%)
    all_gather x1, waiting for transfers between devices, on_device(): lax.all_gather(regrouped[0], 'col', axis=0, tiled=True)  89.1 us
    reduce_scatter x1, waiting for transfers between devices, on_device(): lax.psum_scatter(attn_part[:rows_prompt], 'row', scatter_dimension=1, til...  82.5 us
    all_gather x1, blocking collectives, on_device(): handed = lax.all_gather(packed, 'col', axis=0, tiled=True)  79.5 us
    all_gather x1, blocking collectives, on_device(): returned = lax.all_gather(decode_mixed, 'col', axis=0, tiled=True)  75.5 us
    reduce_scatter x1, waiting for transfers between devices, on_device(): lax.psum_scatter(mlp_part[:rows_prompt].astype(jnp.bfloat16), 'row', scat...  46.9 us
    all_gather x1, waiting for transfers between devices, on_device(): lax.all_gather(prompt_tokens, 'row', axis=1, tiled=True)  44.8 us
    unnamed x11, waiting for transfers between devices  30.9 us
    dot_general x1, matrix products, on_device(): lax.dot_general(hidden, w_reduce, (((1,), (1,)), ((), ())), preferred_ele...  27.6 us
  transfers between devices with their start and end apart: 10, of which 5 were waited for; matrix products, arithmetic and copies ran while one was open for 32% of the time, Pallas kernels for 0%

commit v1 on v0

--- a/solution.py
+++ b/solution.py
@@ -191,7 +191,9 @@
     start_value = own_prob.astype(jnp.float32)[:, :, None] * own_value.astype(jnp.float32)
     decode_sum = lax.fori_loop(0, block_count, value_block, start_value)
     decode_mixed = decode_sum.astype(half_float).reshape(slot_local, heads_local * HD)
-    returned = lax.all_gather(decode_mixed, "col", axis=0, tiled=True)
+    returned = jnp.concatenate(
+        lax.all_to_all(jnp.stack([decode_mixed] * lax.axis_size("col")), "col", 0, 0), axis=0
+    )
     picker = slot_match.astype(half_float)
     decode_heads = jnp.dot(picker, returned, preferred_element_type=jnp.float32).astype(half_float)
     mixed_all = jnp.concatenate([prompt_mixed, decode_heads], axis=0)

time: 751 us -> 675 us (0.90)
  blocking collectives: 185 us -> 110 us
  waiting for transfers between devices: 294 us -> 286 us
    all_gather x1 -> x0, blocking collectives: 75.5 us -> none  [on_device(): returned = lax.all_gather(decode_mixed, 'col', axis=0, tiled=True)]
    unnamed x11, waiting for transfers between devices: 30.9 us -> 22.1 us
    unnamed x34 -> x35, local copies, waits for them, and re-layouts: 21.5 us -> 22.8 us
  transfers between devices with their start and end apart: 10 -> 11, of which waited for: 5 -> 5; matrix products, arithmetic and copies ran while one was open for 32% -> 36% of each run, Pallas kernels for 0% -> 0%
where the time goes in v1:
time: 675 us; the launch traced here: 668 us
  waiting for transfers between devices  286 us (42%)
  local copies, waits for them, and re-layouts  128 us (19%)
  blocking collectives  110 us (16%)
  matrix products  91.6 us (14%)
  other arithmetic  27 us (4%)
  between operations  14.9 us (2%)
  starting transfers between devices  9.66 us (1%)
    all_gather x1, waiting for transfers between devices, on_device(): lax.all_gather(regrouped[0], 'col', axis=0, tiled=True)  89.1 us
    reduce_scatter x1, waiting for transfers between devices, on_device(): lax.psum_scatter(attn_part[:rows_prompt], 'row', scatter_dimension=1, til...  82.5 us
    all_gather x1, blocking collectives, on_device(): handed = lax.all_gather(packed, 'col', axis=0, tiled=True)  79.5 us
    reduce_scatter x1, waiting for transfers between devices, on_device(): lax.psum_scatter(mlp_part[:rows_prompt].astype(jnp.bfloat16), 'row', scat...  47 us
    all_gather x1, waiting for transfers between devices, on_device(): lax.all_gather(prompt_tokens, 'row', axis=1, tiled=True)  44.8 us
    dot_general x1, matrix products, on_device(): lax.dot_general(hidden, w_reduce, (((1,), (1,)), ((), ())), preferred_ele...  27.6 us
    reshape x4, local copies, waits for them, and re-layouts, restore_rows(): block.reshape(col_count, row_count, shard_rows, width).transpose(1, 0, 2, 3)  23.4 us
    unnamed x35, local copies, waits for them, and re-layouts  22.8 us
  transfers between devices with their start and end apart: 11, of which 5 were waited for; matrix products, arithmetic and copies ran while one was open for 36% of the time, Pallas kernels for 0%

profile of v1, /device:TPU:1, one launch (start us, length us, event | category | flops | bytes accessed | tf_op | source)
XLA Modules:
  0.0 667.7 jit_solution(8969276921851607350)
XLA Ops:
  8.1 7.7 %all_to_all.81 = bf16[16,4,512]{2,0,1:T(8,128)(2,1)} all-to-all(bf16[16,4,512]{2,0,1:T(8,128)(2,1)S(1)} %bitcast.184), channel_id=1, replica_groups=mesh['row'=4,'col'=32] {'row'}, dimensions={1} | all-to-all | bytes 131072 | tf_op jit(solution)/shard_map/all_to_all | solution.py:72
  17.7 8.5 %all_to_all.82 = bf16[16,4,1536]{2,0,1:T(8,128)(2,1)} all-to-all(bf16[16,4,1536]{2,0,1:T(8,128)(2,1)S(1)} %bitcast.178), channel_id=1, replica_groups=mesh['row'=4,'col'=32] {'row'}, dimensions={1} | all-to-all | bytes 393216 | tf_op jit(solution)/shard_map/all_to_all | solution.py:69
  27.4 8.8 %all_to_all.83 = bf16[16,4,2048]{2,0,1:T(8,128)(2,1)} all-to-all(bf16[16,4,2048]{2,0,1:T(8,128)(2,1)S(1)} %bitcast.176), channel_id=1, replica_groups=mesh['row'=4,'col'=32] {'row'}, dimensions={1} | all-to-all | bytes 524288 | tf_op jit(solution)/shard_map/all_to_all | solution.py:75
  38.0 4.4 all-to-all-start.4
  42.5 1.3 dynamic_slice.41
  43.8 1.3 dynamic_slice.42
  45.1 2.0 fusion.71
  47.6 6.1 reshape.590
  53.7 11.1 %reshape.562 = bf16[1,8,4096,64]{3,2,1,0:T(8,128)(2,1)} reshape(bf16[2097152]{0:T(1024)(128)(2,1)} %reshape.590) | data formatting | bytes 8388608 | tf_op jit(solution)/shard_map/reshape | solution.py:155
  64.7 6.0 reshape.592
  70.8 11.1 %reshape.563 = bf16[1,8,4096,64]{3,2,1,0:T(8,128)(2,1)} reshape(bf16[2097152]{0:T(1024)(128)(2,1)} %reshape.592) | data formatting | bytes 8388608 | tf_op jit(solution)/shard_map/reshape | solution.py:156
  81.8 5.6 all_gather.22
  88.2 3.2 copy.89
  91.4 44.8 %all-gather.7.cloned.1.call-done = bf16[1024,2048]{1,0:T(8,128)(2,1)} async-done(((bf16[1024,512]{1,0:T(8,128)(2,1)}), bf16[1024,2048]{1,0:T(8,128)(2,1)}) %all-gather.7.cloned.1.call-update) | async-done | bytes 4194320 | tf_op jit(solution)/shard_map/all_gather | solution.py:92
  136.2 2.8 convert_reduce_fusion
  139.1 3.0 fusion.36
  142.2 89.1 %all-gather.9.cloned.1.call-done = bf16[2048,1536]{1,0:T(8,128)(2,1)} async-done(((bf16[64,1536]{1,0:T(8,128)(2,1)}), bf16[2048,1536]{1,0:T(8,128)(2,1)}) %all-gather.9.cloned.1.call-update) | async-done | bytes 6291472 | tf_op jit(solution)/shard_map/all_gather | solution.py:83
  231.2 3.5 copy.76
  235.2 7.0 %fusion.85 = f32[1025,1536]{1,0:T(8,128)S(1)} fusion(bf16[2048,1536]{1,0:T(8,128)(2,1)S(1)} %bitcast.167, f32[2048]{0:T(1024)S(1)} %copy-done.8, f32[2048]{0:T(1024)S(1)} %copy-done.10, f32[1025]{0:T(1024)S(1)} %add_rsqrt_fusion, f32[1025]{0:T(1024)S(1)} %broadcast_multiply_fusion, bf16[1,2048]{1,0:T(2,128)(2,1)S(1)} %all_gather.22, ...), kind=kOutput, calls=%fused_computation.140 | convolution fusion | flops 6467635200 | bytes 16812040 | tf_op jit(solution)/shard_map/dot_general | solution.py:103
  242.2 3.1 slice.161
  245.4 6.6 copy.77
  252.0 9.2 %reshape.557 = f32[2,512,8,3,64]{1,0,4,3,2:T(2,128)} reshape(f32[1024,1536]{0,1:T(8,128)} %copy.77) | data formatting | bytes 12582912 | tf_op jit(solution)/shard_map/reshape | solution.py:129
  261.7 79.5 %all-gather = bf16[32,1,1536]{2,1,0:T(2,128)(2,1)S(1)} all-gather(bf16[1,1,1536]{2,1,0:T(2,128)(2,1)S(1)} %reshape.573), channel_id=1, replica_groups=mesh['row'=4,'col'=32] {'col'}, dimensions={0}, use_global_device_ids=true | all-gather | bytes 101376 | tf_op jit(solution)/shard_map/all_gather | solution.py:147
  341.6 18.7 %while.40 = (s32[]{:T(128)}, f32[1,8,4096]{2,1,0:T(8,128)S(1)}, s32[1]{0:T(128)}, bf16[1,8,4096,64]{3,2,1,0:T(8,128)(2,1)}, bf16[1,8,64]{2,1,0:T(8,128)(2,1)S(1)...) while((s32[]{:T(128)}, f32[1,8,4096]{2,1,0:T(8,128)S(1)}, s32[1]{0:T(128)}, ...), condition=%wide.region_9.10_spmd, body=%wide.region_8.9_spmd.sunk | while | flops 533510 | bytes 1099931 | solution.py:172
  342.3 1.6 fusion.110
  344.7 1.6 fusion.110
  347.0 1.6 fusion.110
  349.3 1.6 fusion.110
  351.7 1.6 fusion.110
  354.0 1.6 fusion.110
  356.4 1.6 fusion.110
  358.7 1.6 fusion.110
  360.9 12.1 %while.41 = (s32[]{:T(128)}, f32[1,8,64]{2,1,0:T(8,128)S(1)}, bf16[1,8,4096]{2,1,0:T(8,128)(2,1)S(1)}, bf16[1,8,4096,64]{3,2,1,0:T(8,128)(2,1)}, s32[]{:T(128)}, /*index=5*/s32[]{:T(128)}, s32[]{:T(128)}, s32[]{:T(128)}) while((s32[]{:T(128)}, f32[1,8,64]{2,1,0:T(8,128)S(1)}, bf16[1,8,4096]{2,1,0:T(8,128)(2,1)S(1)}, ...), condition=%wide.region_13.14_spmd, body=%wide.region_12.13_spmd.sunk | while | flops 524806 | bytes 1081483 | solution.py:192
  360.9 1.5 fusion.113
  362.5 1.5 fusion.113
  364.0 1.5 fusion.113
  365.5 1.5 fusion.113
  367.0 1.5 fusion.113
  368.5 1.5 fusion.113
  370.1 1.5 fusion.113
  371.6 1.5 fusion.113
  375.2 4.5 all-to-all-start.1
  380.0 54.2 %while.42 = (s32[]{:T(128)}, bf16[2,512,512]{2,1,0:T(8,128)(2,1)}, f32[2,512,8,3,64]{1,0,4,3,2:T(2,128)}, s32[2]{0:T(128)}, s32[]{:T(128)}) while((s32[]{:T(128)}, bf16[2,512,512]{2,1,0:T(8,128)(2,1)}, f32[2,512,8,3,64]{1,0,4,3,2:T(2,128)}, s32[2]{0:T(128)}, s32[]{:T(128)}) %tuple.118), condition=%wide.region_5.6_spmd.clone.clone, body=%wide.region_2.5_spmd.clone.clone.sunk | while | flops 554444288 | bytes 41063644 | solution.py:130
  380.0 1.3 dynamic_slice.66
  382.3 6.2 constant_dynamic-slice_fusion.2
  391.6 8.6 %fusion.116 = (f32[8,512]{1,0:T(8,128)}, f32[8,512,512]{1,2,0:T(8,128)}) fusion(pred[512,512]{0,1:T(8,128)(4,1)S(1)} %fusion.115, bf16[512,8,32]{0,2,1:T(8,128)(2,1)} %slice.235, bf16[512,8,16]{0,2,1:T(8,128)(2,1)} %get-tuple-element.479, bf16[512,8,16]{0,2,1:T(8,128)(2,1)} %get-tuple-element.480, bf16[512,8,32]{0,2,1:T(8,128)(2,1)} %slice.236, ...), kind=kOutput, calls=%fused_computation.141.clone.1 | convolution fusion | flops 279970304 | bytes 9715712 | tf_op jit(solution)/shard_map/while/body/eval_jaxpr/sub | solution.py:124
  400.2 5.1 fusion.117
  405.3 1.3 copy.148
  407.4 1.3 dynamic_slice.66
  409.6 6.1 constant_dynamic-slice_fusion.2
  418.8 8.3 %fusion.116 = (f32[8,512]{1,0:T(8,128)}, f32[8,512,512]{1,2,0:T(8,128)}) fusion(pred[512,512]{0,1:T(8,128)(4,1)S(1)} %fusion.115, bf16[512,8,32]{0,2,1:T(8,128)(2,1)} %slice.235, bf16[512,8,16]{0,2,1:T(8,128)(2,1)} %get-tuple-element.479, bf16[512,8,16]{0,2,1:T(8,128)(2,1)} %get-tuple-element.480, bf16[512,8,32]{0,2,1:T(8,128)(2,1)} %slice.236, ...), kind=kOutput, calls=%fused_computation.141.clone.1 | convolution fusion | flops 279970304 | bytes 9715712 | tf_op jit(solution)/shard_map/while/body/eval_jaxpr/sub | solution.py:124
  427.1 5.1 fusion.117
  435.8 4.3 fusion.53
  440.1 3.3 copy-done.1
  443.5 1.3 copy.99
  445.1 8.4 %copy.91 = bf16[32,4,16,2048]{3,2,0,1:T(8,128)(2,1)} copy(bf16[32,4,16,2048]{3,2,1,0:T(8,128)(2,1)} %bitcast.162) | data formatting | bytes 16777216 | tf_op jit(solution)/shard_map/reshape | solution.py:44
  453.6 8.4 %copy.93 = bf16[32,4,16,2048]{3,2,0,1:T(8,128)(2,1)} copy(bf16[32,4,16,2048]{3,2,1,0:T(8,128)(2,1)} %bitcast.163) | data formatting | bytes 16777216 | tf_op jit(solution)/shard_map/reshape | solution.py:44
  461.9 27.6 %convolution_convert_fusion = bf16[1025,2048]{1,0:T(8,128)(2,1)} fusion(bf16[2048,2048]{1,0:T(8,128)(2,1)} %bitcast.165, bf16[2048,2048]{1,0:T(8,128)(2,1)} %bitcast.164, f32[2048]{0:T(1024)S(1)} %copy-done.9, f32[2048]{0:T(1024)S(1)} %copy-done.11, f32[1025]{0:T(1024)S(1)} %copy-done.5, f32[1025]{0:T(1024)S(1)} %broadcast_multiply_fusion, ...), kind=kOutput, calls=%fused_computation.73 | convolution fusion | flops 17236531200 | bytes 25198600 | tf_op jit(solution)/shard_map/dot_general | solution.py:107
  491.5 4.7 slice.170
  496.3 7.8 %slice.169 = f32[1024,2048]{1,0:T(8,128)} slice(f32[1025,2048]{1,0:T(8,128)} %copy-done.1), slice={[0:1024], [0:2048]} | slice | bytes 16777216 | tf_op jit(solution)/shard_map/slice | solution.py:204
  505.3 21.3 %reduce-scatter.15.cloned.1.call-done = bf16[512,1]{1,0:T(8,128)(2,1)} async-done(((bf16[2048,1]{1,0:T(8,128)(2,1)}), bf16[512,1]{1,0:T(8,128)(2,1)}) %reduce-scatter.15.cloned.1.call-update) | async-done | bytes 1040
  528.2 47.0 %reduce-scatter.11.cloned.1.call-done = bf16[1024,512]{1,0:T(8,128)(2,1)} async-done(((bf16[1024,2048]{1,0:T(8,128)(2,1)}), bf16[1024,512]{1,0:T(8,128)(2,1)}) %reduce-scatter.11.cloned.1.call-update) | async-done | bytes 1048592 | tf_op jit(solution)/shard_map/reduce_scatter | solution.py:208
  575.2 82.5 %reduce-scatter.9.cloned.1.call-done = f32[1024,512]{1,0:T(8,128)} async-done(((f32[1024,2048]{1,0:T(8,128)}), f32[1024,512]{1,0:T(8,128)}) %reduce-scatter.9.cloned.1.call-update) | async-done | bytes 2097168 | tf_op jit(solution)/shard_map/reduce_scatter | solution.py:204
  657.7 3.3 add_convert_fusion.2
  (160 shorter events, 34.4 us)
Async XLA Ops:
  7.2 81.0 %all-gather.11.cloned.1.call-start = ((), (), s32[]{:S(2)}) async-start(), calls=%async_computation.11 | async-start | bytes 2162688 | tf_op jit(solution)/shard_map/all_gather | solution.py:84
  15.9 120.4 %all-gather.7.cloned.1.call-start = ((), (), s32[]{:S(2)}) async-start(), calls=%async_computation.9 | async-start | bytes 5242880 | tf_op jit(solution)/shard_map/all_gather | solution.py:92
  16.6 214.6 %all-gather.9.cloned.1.call-start = ((), (), s32[]{:S(2)}) async-start(), calls=%async_computation.10 | async-start | bytes 6488064 | tf_op jit(solution)/shard_map/all_gather | solution.py:83
  26.3 418.9 %all-gather.13.cloned.1.call-start = ((), (), s32[]{:S(2)}) async-start(), calls=%async_computation.13 | async-start | bytes 8650752 | tf_op jit(solution)/shard_map/all_gather | solution.py:85
  38.0 49.4 %all-to-all-start.4 = ((bf16[16,4,2048]{2,0,1:T(8,128)(2,1)}), bf16[16,4,2048]{2,0,1:T(8,128)(2,1)S(1)}, u32[]{:S(2)}, u32[]{:S(2)}) async-start(bf16[16,4,2048]{2,0,1:T(8,128)(2,1)} %bitcast.127), calls=%async_computation.5 | async-start | bytes 524288 | tf_op jit(solution)/shard_map/all_to_all | solution.py:78
  42.5 411.1 %all-gather.15.cloned.1.call-start = ((), (), s32[]{:S(2)}) async-start(), calls=%async_computation.14 | async-start | bytes 8650752 | tf_op jit(solution)/shard_map/all_gather | solution.py:86
  64.7 17.1 %copy-start.6 = (bf16[1,512]{1,0:T(2,128)(2,1)S(1)}, bf16[1,512]{1,0:T(2,128)(2,1)}, u32[]{:S(2)}) copy-start(bf16[1,512]{1,0:T(2,128)(2,1)} %param.20) | copy-start | bytes 3076
  87.5 0.7 copy-start.3
  139.1 95.6 %copy-start.8 = (f32[2048]{0:T(1024)S(1)}, f32[2048]{0:T(1024)}, u32[]{:S(2)}) copy-start(f32[2048]{0:T(1024)} %param.22) | copy-start | bytes 24580
  139.1 95.6 %copy-start.10 = (f32[2048]{0:T(1024)S(1)}, f32[2048]{0:T(1024)}, u32[]{:S(2)}) copy-start(f32[2048]{0:T(1024)} %param.21) | copy-start | bytes 24580
  142.1 92.5 %copy-start.4 = (f32[1025]{0:T(1024)}, f32[1025]{0:T(1024)S(1)}, u32[]{:S(2)}) copy-start(f32[1025]{0:T(1024)S(1)} %add_rsqrt_fusion) | copy-start | bytes 12304
  231.2 4.0 copy-start
  252.0 89.2 %copy-start.12 = (s32[32]{0:T(128)S(1)}, s32[32]{0:T(128)}, u32[]{:S(2)}) copy-start(s32[32]{0:T(128)} %param.31) | copy-start | bytes 388
  375.2 59.0 %all-to-all-start.1 = ((bf16[32,2,256]{2,1,0:T(2,128)(2,1)}), bf16[32,2,256]{2,1,0:T(2,128)(2,1)}, u32[]{:S(2)}, u32[]{:S(2)}) async-start(bf16[32,2,256]{2,1,0:T(2,128)(2,1)} %reshape.594), calls=%async_computation.1 | async-start | bytes 65536 | tf_op jit(solution)/shard_map/all_to_all | solution.py:195
  379.8 124.4 %reduce-scatter.13.cloned.1.call-start = ((), (), s32[]{:S(2)}) async-start(), calls=%async_computation.16 | async-start | bytes 1310720
  440.1 3.3 copy-start.1
  444.9 81.7 %reduce-scatter.15.cloned.1.call-start = ((), (), s32[]{:S(2)}) async-start(), calls=%async_computation.17 | async-start | bytes 655360
  453.6 8.4 %copy-start.5 = (f32[1025]{0:T(1024)S(1)}, f32[1025]{0:T(1024)}, u32[]{:S(2)}) copy-start(f32[1025]{0:T(1024)} %copy-done.4) | copy-start | bytes 12304
  453.6 8.4 %copy-start.9 = (f32[2048]{0:T(1024)S(1)}, f32[2048]{0:T(1024)}, u32[]{:S(2)}) copy-start(f32[2048]{0:T(1024)} %param.22) | copy-start | bytes 24580
  453.6 8.4 %copy-start.11 = (f32[2048]{0:T(1024)S(1)}, f32[2048]{0:T(1024)}, u32[]{:S(2)}) copy-start(f32[2048]{0:T(1024)} %param.21) | copy-start | bytes 24580
  491.4 83.8 %reduce-scatter.11.cloned.1.call-start = ((), (), s32[]{:S(2)}) async-start(), calls=%async_computation.15 | async-start | bytes 5242880 | tf_op jit(solution)/shard_map/reduce_scatter | solution.py:208
  496.2 161.5 %reduce-scatter.9.cloned.1.call-start = ((), (), s32[]{:S(2)}) async-start(), calls=%async_computation.12 | async-start | bytes 10485760 | tf_op jit(solution)/shard_map/reduce_scatter | solution.py:204
  504.1 23.5 %copy-start.7 = (bf16[1,512]{1,0:T(2,128)(2,1)S(1)}, bf16[1,512]{1,0:T(2,128)(2,1)}, u32[]{:S(2)}) copy-start(bf16[1,512]{1,0:T(2,128)(2,1)} %param.20) | copy-start | bytes 3076
  504.1 153.6 %copy-start.2 = (bf16[1024,512]{1,0:T(8,128)(2,1)S(1)}, bf16[1024,512]{1,0:T(8,128)(2,1)}, u32[]{:S(2)}) copy-start(bf16[1024,512]{1,0:T(8,128)(2,1)} %param.19) | copy-start | bytes 3145732
Sparse Core Ops, SparseCore 0:
  16.0 71.9 all-gather.10
  89.7 46.5 all-gather.6
  139.2 91.9 all-gather.8
  234.2 104.0 all-gather.12
  341.4 101.3 all-gather.14
  445.6 36.1 reduce-scatter.12
  491.6 34.9 reduce-scatter.14
  529.1 46.0 reduce-scatter.10
  577.7 79.9 reduce-scatter.8
